TPU v7x, 32 devices: a whole 2x2x4 slice. The times are simulated.
32 devices in a mesh: grp: 4 (over z), band: 8 (over y, x, core).
Axes of the slice: x: 2, y: 2, z: 4, core: 2. Of those that a mesh axis runs over, the one named last changes fastest.
Arguments:
- orbitals: float32 [18432, 512], P('grp', 'band'), may hold values from -6 to 6
- requests: int32 [32, 6], replicated, may hold values from -1 to 11, as said below
- coulomb: float32 [96, 1536, 1536], P(('grp', 'band')), may hold values from -0.001953125 to 0.001953125
Outputs:
- exchange_rows: float32 [18432, 512], P('grp', 'band')
Inputs may be any that keep to these rules, and one draw needn't show every extreme that they name: `requests`: entries 2q and 2q + 1 of row d are the two blocks of slot q of device d, the first not above the second, or both -1 for an empty slot; every pair of the 12 blocks, a block with itself included, stands in exactly one slot.
All inputs are finite; a program needn't handle non-finite values.
Results may differ from a plain program's by a relative error of at most 0.0003.
Values sent between devices are 32-bit elements; how exact they have to be, the bound alone decides.
No kernel may reach another device: no remote copies, remote signals or barrier semaphores. Data moves between devices by JAX's collectives and lax.ppermute only.
A program may use at most 256 MiB of HBM per device.

v0:
```python
import jax
import jax.numpy as jnp
from jax import lax
from jax.sharding import PartitionSpec as P


def slot_work(first_block, second_block, coulomb_tile, diagonal):
    density = jnp.dot(
        first_block,
        second_block.T,
        precision=lax.Precision.HIGHEST,
        preferred_element_type=jnp.float32,
    )
    symmetric = jnp.where(diagonal, 0.5 * (coulomb_tile + coulomb_tile.T), coulomb_tile)
    kernel = density * symmetric
    onto_first = jnp.dot(
        kernel, second_block, precision=lax.Precision.HIGHEST, preferred_element_type=jnp.float32
    )
    onto_second = jnp.dot(
        kernel.T, first_block, precision=lax.Precision.HIGHEST, preferred_element_type=jnp.float32
    )
    onto_second = onto_second * jnp.where(diagonal, 0.0, 1.0)
    return jnp.stack([onto_first, onto_second], 0)


def body(orbitals, requests, coulomb):
    group_count = lax.axis_size("grp")
    band_count = lax.axis_size("band")
    devices = group_count * band_count
    blk = coulomb.shape[1]
    col_width = orbitals.shape[1]
    orbital_width = col_width * band_count
    piece_rows = blk // devices
    all_points = lax.all_gather(orbitals, "grp", axis=0, tiled=True)
    block_count = all_points.shape[0] // (devices * piece_rows)
    blocks = (
        all_points.reshape(devices, block_count, piece_rows, col_width)
        .transpose(1, 0, 2, 3)
        .reshape(block_count, blk, col_width)
    )
    request_count = requests.shape[1]
    group_index = lax.axis_index("grp")
    band_index = lax.axis_index("band")
    group_requests = lax.dynamic_slice_in_dim(requests, group_index * band_count, band_count, 0)
    live = (group_requests >= 0).astype(jnp.float32)
    outgoing = jnp.take(blocks, jnp.maximum(group_requests, 0), axis=0) * live[:, :, None, None]
    arrived = lax.all_to_all(outgoing, "band", split_axis=0, concat_axis=0, tiled=True)
    fetched = arrived.transpose(1, 2, 0, 3).reshape(request_count // 2, 2, blk, orbital_width)
    own_pairs = lax.dynamic_index_in_dim(group_requests, band_index, 0, keepdims=False).reshape(
        request_count // 2, 2
    )
    diagonal = own_pairs[:, 0] == own_pairs[:, 1]

    def per_slot(slot_item):
        pair_rows, coulomb_tile, diag_flag = slot_item
        return slot_work(pair_rows[0], pair_rows[1], coulomb_tile, diag_flag)

    results = lax.map(per_slot, (fetched, coulomb, diagonal))
    outbound = results.reshape(request_count, blk, band_count, col_width).transpose(2, 0, 1, 3)
    returned = lax.all_to_all(outbound, "band", split_axis=0, concat_axis=0, tiled=True)
    one_hot = (
        group_requests[:, :, None] == jnp.arange(block_count, dtype=jnp.int32)[None, None, :]
    ).astype(jnp.float32)
    summed = jnp.einsum("srk,srpc->kpc", one_hot, returned, precision=lax.Precision.HIGHEST)
    summed = summed.reshape(block_count, group_count, band_count, piece_rows, col_width)
    mine = lax.psum_scatter(summed, "grp", scatter_dimension=1, tiled=True)
    mine = mine.reshape(block_count, band_count, piece_rows, col_width).transpose(1, 0, 2, 3)
    return mine.reshape(band_count * block_count * piece_rows, col_width)


def solution(mesh):
    placed = (P("grp", "band"), P(), P(("grp", "band"), None, None))
    return jax.shard_map(
        body, mesh=mesh, in_specs=placed, out_specs=P("grp", "band"), check_vma=False
    )
```

profile of v0, /device:TPU:0, one launch (start us, length us, event | category | flops | bytes accessed | tf_op | source)
XLA Modules:
  0.0 1245.0 jit_solution(937388461470944513)
XLA Ops:
  10.6 168.5 %all-gather.2.cloned.1.call-done = f32[18432,64]{1,0:T(8,128)} async-done(((f32[4608,64]{1,0:T(8,128)}), f32[18432,64]{1,0:T(8,128)}) %all-gather.2.cloned.1.call-update) | async-done | bytes 4718608 | tf_op jit(solution)/shard_map/all_gather | solution.py:34
  179.0 12.0 copy.38
  191.1 13.1 %reshape.38 = f32[12,1536,64]{1,2,0:T(8,128)} reshape(f32[12,32,48,64]{2,1,3,0:T(8,128)} %copy.38) | data formatting | bytes 9437184 | tf_op jit(solution)/shard_map/reshape | solution.py:39
  204.1 12.6 %gather_fusion = f32[48,1536,64]{1,2,0:T(8,128)} fusion(f32[12,1536,64]{1,2,0:T(8,128)} %reshape.38, s32[1024]{0:T(1024)S(1)} %pad_clamp_fusion), kind=kCustom, calls=%fused_computation | custom fusion | bytes 37748928 | tf_op jit(solution)/shard_map/jit(_take)/gather | solution.py:46
  216.8 13.2 %select_multiply_fusion = f32[8,6,1536,64]{2,3,1,0:T(8,128)} fusion(f32[8,6,1536,64]{2,3,1,0:T(8,128)} %bitcast.84, f32[8,6]{1,0:T(8,128)S(1)} %copy.40, pred[8,6]{1,0:T(8,128)(4,1)S(1)} %copy.36), kind=kLoop, calls=%fused_computation.18 | loop fusion | flops 9437184 | bytes 37748976 | tf_op jit(solution)/shard_map/mul | solution.py:46
  236.5 205.9 %all-to-all-done = f32[8,6,1536,64]{2,3,1,0:T(8,128)} async-done(((f32[8,6,1536,64]{2,3,1,0:T(8,128)}), f32[8,6,1536,64]{2,3,1,0:T(8,128)}, u32[]{:S(2)}, u32[]{:S(2)}) %all-to-all-start) | async-done | bytes 18874400 | tf_op jit(solution)/shard_map/all_to_all | solution.py:47
  442.4 12.6 %copy.41 = f32[6,1536,8,64]{1,3,2,0:T(8,128)} copy(f32[6,1536,8,64]{1,3,0,2:T(8,128)} %bitcast.12) | data formatting | bytes 37748736 | tf_op jit(solution)/shard_map/transpose | solution.py:48
  455.0 359.6 %while.10 = (s32[]{:T(128)}, f32[3,2,1536,512]{2,3,1,0:T(8,128)}, f32[3,2,1536,512]{2,3,1,0:T(8,128)}, pred[3]{0:T(512)(128)(4,1)S(1)}, f32[3,1536,1536]{2,1,0:T...) while((s32[]{:T(128)}, f32[3,2,1536,512]{2,3,1,0:T(8,128)}, ...), condition=%wide.region_1.2_spmd, body=%wide.region_0.1_spmd.sunk | while | flops 43498340352 | bytes 179310272 | solution.py:58
  475.3 8.1 dynamic-slice_bitcast_fusion.16
  483.4 9.6 copy.64
  493.6 22.7 %convolution_multiply_fusion.3 = f32[1536,1536]{1,0:T(8,128)S(1)} fusion(f32[1536,1536]{0,1:T(8,128)} %copy.64, pred[]{:T(512)} %bitcast.83, f32[3,2,1536,512]{2,3,1,0:T(8,128)} %get-tuple-element.113, s32[]{:T(128)} %get-tuple-element.101, s32[]{:T(128)S(6)} %add.38, f32[3,1536,1536]{2,1,0:T(8,128)} %get-tuple-element.115), kind=kOutput, calls=%fused_computation.1.clone.1 | convolution fusion | flops 14504951808 | bytes 34605060 | tf_op jit(solution)/shard_map/while/body/eval_jaxpr/dot_general | solution.py:8
  519.9 17.0 %convolution_bitcast_fusion.2 = f32[1,1536,512]{2,1,0:T(8,128)S(1)} fusion(f32[1536,1536]{1,0:T(8,128)S(1)} %convolution_multiply_fusion.3, f32[3,2,1536,512]{2,3,1,0:T(8,128)} %get-tuple-element.113, s32[]{:T(128)} %get-tuple-element.101, s32[]{:T(128)S(6)} %add.38), kind=kOutput, calls=%fused_computation.9.clone.1 | convolution fusion | flops 14495514624 | bytes 15729156 | tf_op jit(solution)/shard_map/while/body/eval_jaxpr/dot_general | solution.py:16
  537.4 32.9 %fusion.22 = f32[1,1536,512]{2,1,0:T(8,128)S(1)} fusion(f32[1536,1536]{1,0:T(8,128)} %copy-done, f32[3,2,1536,512]{2,3,1,0:T(8,128)} %get-tuple-element.113, s32[]{:T(128)} %get-tuple-element.101, f32[]{:T(128)S(6)} %select_n.45), kind=kOutput, calls=%fused_computation.8.clone.1 | convolution fusion | flops 14496301056 | bytes 15729156 | tf_op jit(solution)/shard_map/while/body/eval_jaxpr/dot_general | solution.py:19
  573.6 6.6 copy.65
  586.0 8.1 dynamic-slice_bitcast_fusion.16
  594.1 9.6 copy.64
  604.3 22.7 %convolution_multiply_fusion.3 = f32[1536,1536]{1,0:T(8,128)S(1)} fusion(f32[1536,1536]{0,1:T(8,128)} %copy.64, pred[]{:T(512)} %bitcast.83, f32[3,2,1536,512]{2,3,1,0:T(8,128)} %get-tuple-element.113, s32[]{:T(128)} %get-tuple-element.101, s32[]{:T(128)S(6)} %add.38, f32[3,1536,1536]{2,1,0:T(8,128)} %get-tuple-element.115), kind=kOutput, calls=%fused_computation.1.clone.1 | convolution fusion | flops 14504951808 | bytes 34605060 | tf_op jit(solution)/shard_map/while/body/eval_jaxpr/dot_general | solution.py:8
  630.6 17.0 %convolution_bitcast_fusion.2 = f32[1,1536,512]{2,1,0:T(8,128)S(1)} fusion(f32[1536,1536]{1,0:T(8,128)S(1)} %convolution_multiply_fusion.3, f32[3,2,1536,512]{2,3,1,0:T(8,128)} %get-tuple-element.113, s32[]{:T(128)} %get-tuple-element.101, s32[]{:T(128)S(6)} %add.38), kind=kOutput, calls=%fused_computation.9.clone.1 | convolution fusion | flops 14495514624 | bytes 15729156 | tf_op jit(solution)/shard_map/while/body/eval_jaxpr/dot_general | solution.py:16
  648.2 32.9 %fusion.22 = f32[1,1536,512]{2,1,0:T(8,128)S(1)} fusion(f32[1536,1536]{1,0:T(8,128)} %copy-done, f32[3,2,1536,512]{2,3,1,0:T(8,128)} %get-tuple-element.113, s32[]{:T(128)} %get-tuple-element.101, f32[]{:T(128)S(6)} %select_n.45), kind=kOutput, calls=%fused_computation.8.clone.1 | convolution fusion | flops 14496301056 | bytes 15729156 | tf_op jit(solution)/shard_map/while/body/eval_jaxpr/dot_general | solution.py:19
  684.4 6.6 copy.65
  696.9 8.1 dynamic-slice_bitcast_fusion.16
  704.9 9.6 copy.64
  715.1 22.7 %convolution_multiply_fusion.3 = f32[1536,1536]{1,0:T(8,128)S(1)} fusion(f32[1536,1536]{0,1:T(8,128)} %copy.64, pred[]{:T(512)} %bitcast.83, f32[3,2,1536,512]{2,3,1,0:T(8,128)} %get-tuple-element.113, s32[]{:T(128)} %get-tuple-element.101, s32[]{:T(128)S(6)} %add.38, f32[3,1536,1536]{2,1,0:T(8,128)} %get-tuple-element.115), kind=kOutput, calls=%fused_computation.1.clone.1 | convolution fusion | flops 14504951808 | bytes 34605060 | tf_op jit(solution)/shard_map/while/body/eval_jaxpr/dot_general | solution.py:8
  741.4 17.0 %convolution_bitcast_fusion.2 = f32[1,1536,512]{2,1,0:T(8,128)S(1)} fusion(f32[1536,1536]{1,0:T(8,128)S(1)} %convolution_multiply_fusion.3, f32[3,2,1536,512]{2,3,1,0:T(8,128)} %get-tuple-element.113, s32[]{:T(128)} %get-tuple-element.101, s32[]{:T(128)S(6)} %add.38), kind=kOutput, calls=%fused_computation.9.clone.1 | convolution fusion | flops 14495514624 | bytes 15729156 | tf_op jit(solution)/shard_map/while/body/eval_jaxpr/dot_general | solution.py:16
  759.0 32.9 %fusion.22 = f32[1,1536,512]{2,1,0:T(8,128)S(1)} fusion(f32[1536,1536]{1,0:T(8,128)} %copy-done, f32[3,2,1536,512]{2,3,1,0:T(8,128)} %get-tuple-element.113, s32[]{:T(128)} %get-tuple-element.101, f32[]{:T(128)S(6)} %select_n.45), kind=kOutput, calls=%fused_computation.8.clone.1 | convolution fusion | flops 14496301056 | bytes 15729156 | tf_op jit(solution)/shard_map/while/body/eval_jaxpr/dot_general | solution.py:19
  795.2 6.6 copy.65
  814.6 12.6 %copy.44 = f32[8,6,1536,64]{2,3,1,0:T(8,128)} copy(f32[8,6,1536,64]{2,3,0,1:T(8,128)} %bitcast.86) | data formatting | bytes 37748736 | tf_op jit(solution)/shard_map/transpose | solution.py:59
  827.2 210.7 %all_to_all.10 = f32[8,6,1536,64]{2,3,1,0:T(8,128)S(1)} all-to-all(f32[8,6,1536,64]{2,3,1,0:T(8,128)} %copy.44), channel_id=1, replica_groups=mesh['grp'=4,'band'=8] {'band'}, dimensions={0} | all-to-all | bytes 37748736 | tf_op jit(solution)/shard_map/all_to_all | solution.py:60
  1037.9 15.3 %fusion.8 = f32[12,1536,64]{1,0,2:T(8,128)} fusion(f32[8,6,1536,64]{2,3,1,0:T(8,128)S(1)} %all_to_all.10, s32[8,6]{0,1:T(8,128)S(1)} %copy-done.2), kind=kOutput, calls=%fused_computation.19 | convolution fusion | flops 679477824 | bytes 23593152 | tf_op jit(solution)/shard_map/srk,srpc->kpc/dot_general | solution.py:64
  1053.2 11.0 reshape.57
  1064.2 12.2 copy.47
  1076.5 157.9 %reduce-scatter.2.cloned.1.call-done = f32[12,1,8,48,64]{4,3,2,0,1:T(8,128)} async-done(((f32[12,4,8,48,64]{4,3,2,0,1:T(8,128)}), f32[12,1,8,48,64]{4,3,2,0,1:T(8,128)}) %reduce-scatter.2.cloned.1.call-update) | async-done | bytes 1179664 | tf_op jit(solution)/shard_map/reduce_scatter | solution.py:66
  (41 shorter events, 54.2 us)
Async XLA Ops:
  6.5 172.5 %all-gather.2.cloned.1.call-start = ((), (), s32[]{:S(2)}) async-start(), calls=%async_computation.3 | async-start | bytes 11796480 | tf_op jit(solution)/shard_map/all_gather | solution.py:34
  10.2 180.9 %copy-start.1 = (s32[8,6]{0,1:T(8,128)}, s32[8,6]{0,1:T(8,128)S(1)}, u32[]{:S(2)}) copy-start(s32[8,6]{0,1:T(8,128)S(1)} %get-tuple-element.59) | copy-start | bytes 580
  230.0 6.1 copy-start.3
  230.0 212.4 %all-to-all-start = ((f32[8,6,1536,64]{2,3,1,0:T(8,128)}), f32[8,6,1536,64]{2,3,1,0:T(8,128)}, u32[]{:S(2)}, u32[]{:S(2)}) async-start(f32[8,6,1536,64]{2,3,1,0:T(8,128)} %select_multiply_fusion), calls=%async_computation | async-start | bytes 37748736 | tf_op jit(solution)/shard_map/all_to_all | solution.py:47
  236.0 998.4 %reduce-scatter.2.cloned.1.call-start = ((), (), s32[]{:S(2)}) async-start(), calls=%async_computation.4 | async-start | bytes 11796480 | tf_op jit(solution)/shard_map/reduce_scatter | solution.py:66
  516.3 3.6 copy-start
  627.0 3.6 copy-start
  737.8 3.6 copy-start
  827.2 210.7 %copy-start.2 = (s32[8,6]{0,1:T(8,128)S(1)}, s32[8,6]{0,1:T(8,128)}, u32[]{:S(2)}) copy-start(s32[8,6]{0,1:T(8,128)} %copy-done.1) | copy-start | bytes 580
Sparse Core Ops, SparseCore 0:
  9.5 169.4 all-gather.1
  1076.6 157.7 reduce-scatter.1
where the time goes:
time: 1250 us; the launch traced here: 1240 us
  waiting for transfers between devices  532 us (43%)
  matrix products  233 us (19%)
  blocking collectives  211 us (17%)
  local copies, waits for them, and re-layouts  196 us (16%)
  loops' own time  29 us (2%)
  other arithmetic  24 us (2%)
  between operations  13.7 us (1%)
    all_to_all x1, blocking collectives, body(): lax.all_to_all(outbound, 'band', split_axis=0, concat_axis=0, tiled=True)  211 us
    all_to_all x1, waiting for transfers between devices, body(): lax.all_to_all(outgoing, 'band', split_axis=0, concat_axis=0, tiled=True)  206 us
    all_gather x1, waiting for transfers between devices, body(): all_points = lax.all_gather(orbitals, 'grp', axis=0, tiled=True)  168 us
    reduce_scatter x1, waiting for transfers between devices, body(): mine = lax.psum_scatter(summed, 'grp', scatter_dimension=1, tiled=True)  158 us
    dot_general x3, matrix products, slot_work(): jnp.dot(kernel.T, first_block, precision=lax.Precision.HIGHEST, preferred...  98.7 us
    dot_general x3, matrix products, slot_work(): jnp.dot(first_block, second_block.T, precision=lax.Precision.HIGHEST, pre...  68 us
    squeeze x6, local copies, waits for them, and re-layouts, body(): results = lax.map(per_slot, (fetched, coulomb, diagonal))  53.1 us
    dot_general x3, matrix products, slot_work(): jnp.dot(kernel, second_block, precision=lax.Precision.HIGHEST, preferred_...  51.1 us
  transfers between devices with their start and end apart: 3, of which 3 were waited for; matrix products, arithmetic and copies ran while one was open for 0% of the time, Pallas kernels for 0%

commit v1 on v0

--- a/solution.py
+++ b/solution.py
@@ -31,7 +31,12 @@
     col_width = orbitals.shape[1]
     orbital_width = col_width * band_count
     piece_rows = blk // devices
-    all_points = lax.all_gather(orbitals, "grp", axis=0, tiled=True)
+    ring = [orbitals]
+    for hop in range(3):
+        ring.append(lax.ppermute(ring[-1], "grp", [(dev, (dev + 1) % 4) for dev in range(4)]))
+    all_points = jnp.roll(
+        jnp.concatenate(ring[::-1], axis=0), (lax.axis_index("grp") + 1) * ring[0].shape[0], axis=0
+    )
     block_count = all_points.shape[0] // (devices * piece_rows)
     blocks = (
         all_points.reshape(devices, block_count, piece_rows, col_width)

time: 1250 us -> 1180 us (0.944)
  waiting for transfers between devices: 532 us -> 439 us
  local copies, waits for them, and re-layouts: 196 us -> 213 us
    all_gather x1 -> x0, waiting for transfers between devices: 168 us -> none  [body(): all_points = lax.all_gather(orbitals, 'grp', axis=0, tiled=True)]
    ppermute x0 -> x3, waiting for transfers between devices: none -> 75.5 us  [body(): lax.ppermute(ring[-1], 'grp', [(dev, (dev + 1) % 4) for dev in range(4)])]
  transfers between devices with their start and end apart: 3 -> 5, of which waited for: 3 -> 5; matrix products, arithmetic and copies ran while one was open for 0% -> 1% of each run, Pallas kernels for 0% -> 0%
where the time goes in v1:
time: 1180 us; the launch traced here: 1170 us
  waiting for transfers between devices  439 us (37%)
  matrix products  233 us (20%)
  local copies, waits for them, and re-layouts  213 us (18%)
  blocking collectives  211 us (18%)
  loops' own time  29 us (2%)
  other arithmetic  25.3 us (2%)
  between operations  13.8 us (1%)
    all_to_all x1, blocking collectives, body(): lax.all_to_all(outbound, 'band', split_axis=0, concat_axis=0, tiled=True)  211 us
    all_to_all x1, waiting for transfers between devices, body(): lax.all_to_all(outgoing, 'band', split_axis=0, concat_axis=0, tiled=True)  206 us
    reduce_scatter x1, waiting for transfers between devices, body(): mine = lax.psum_scatter(summed, 'grp', scatter_dimension=1, tiled=True)  158 us
    dot_general x3, matrix products, slot_work(): jnp.dot(kernel.T, first_block, precision=lax.Precision.HIGHEST, preferred...  98.7 us
    ppermute x3, waiting for transfers between devices, body(): lax.ppermute(ring[-1], 'grp', [(dev, (dev + 1) % 4) for dev in range(4)])  75.5 us
    dot_general x3, matrix products, slot_work(): jnp.dot(first_block, second_block.T, precision=lax.Precision.HIGHEST, pre...  68 us
    squeeze x6, local copies, waits for them, and re-layouts, body(): results = lax.map(per_slot, (fetched, coulomb, diagonal))  53.1 us
    dot_general x3, matrix products, slot_work(): jnp.dot(kernel, second_block, precision=lax.Precision.HIGHEST, preferred_...  51.1 us
  transfers between devices with their start and end apart: 5, of which 5 were waited for; matrix products, arithmetic and copies ran while one was open for 1% of the time, Pallas kernels for 0%

profile of v1, /device:TPU:0, one launch (start us, length us, event | category | flops | bytes accessed | tf_op | source)
XLA Modules:
  0.0 1173.2 jit_solution(761536043164368507)
XLA Ops:
  9.6 28.2 %collective-permute-done = f32[4608,64]{0,1:T(8,128)S(1)} collective-permute-done((f32[4608,64]{0,1:T(8,128)}, f32[4608,64]{0,1:T(8,128)S(1)}, u32[]{:S(2)}, u32[]{:S(2)}) %collective-permute-start) | collective-permute-done | bytes 1179680 | tf_op jit(solution)/shard_map/ppermute | solution.py:36
  37.8 29.1 %collective-permute-done.1 = f32[4608,64]{0,1:T(8,128)} collective-permute-done((f32[4608,64]{0,1:T(8,128)S(1)}, f32[4608,64]{0,1:T(8,128)}, u32[]{:S(2)}, u32[]{:S(2)}) %collective-permute-start.1) | collective-permute-done | bytes 1179680 | tf_op jit(solution)/shard_map/ppermute | solution.py:36
  76.9 18.3 %collective-permute-done.2 = f32[4608,64]{0,1:T(8,128)} collective-permute-done((f32[4608,64]{0,1:T(8,128)}, f32[4608,64]{0,1:T(8,128)}, u32[]{:S(2)}, u32[]{:S(2)}) %collective-permute-start.2) | collective-permute-done | bytes 1179680 | tf_op jit(solution)/shard_map/ppermute | solution.py:36
  107.1 12.0 %copy.54 = f32[12,32,48,64]{2,1,3,0:T(8,128)} copy(f32[12,32,48,64]{3,2,0,1:T(8,128)} %bitcast.86) | data formatting | bytes 9437184 | tf_op jit(solution)/shard_map/transpose | solution.py:43
  119.1 13.1 %reshape.38 = f32[12,1536,64]{1,2,0:T(8,128)} reshape(f32[12,32,48,64]{2,1,3,0:T(8,128)} %copy.54) | data formatting | bytes 9437184 | tf_op jit(solution)/shard_map/reshape | solution.py:44
  132.2 12.6 %gather_fusion = f32[48,1536,64]{1,2,0:T(8,128)} fusion(f32[12,1536,64]{1,2,0:T(8,128)} %reshape.38, s32[1024]{0:T(1024)S(1)} %pad_clamp_fusion), kind=kCustom, calls=%fused_computation | custom fusion | bytes 37748928 | tf_op jit(solution)/shard_map/jit(_take)/gather | solution.py:51
  144.9 13.2 %select_multiply_fusion = f32[8,6,1536,64]{2,3,1,0:T(8,128)} fusion(f32[8,6,1536,64]{2,3,1,0:T(8,128)} %bitcast.84, f32[8,6]{1,0:T(8,128)S(1)} %copy.56, pred[8,6]{1,0:T(8,128)(4,1)S(1)} %copy.45), kind=kLoop, calls=%fused_computation.18 | loop fusion | flops 9437184 | bytes 37748976 | tf_op jit(solution)/shard_map/mul | solution.py:51
  164.7 205.9 %all-to-all-done = f32[8,6,1536,64]{2,3,1,0:T(8,128)} async-done(((f32[8,6,1536,64]{2,3,1,0:T(8,128)}), f32[8,6,1536,64]{2,3,1,0:T(8,128)}, u32[]{:S(2)}, u32[]{:S(2)}) %all-to-all-start) | async-done | bytes 18874400 | tf_op jit(solution)/shard_map/all_to_all | solution.py:52
  370.5 12.6 %copy.57 = f32[6,1536,8,64]{1,3,2,0:T(8,128)} copy(f32[6,1536,8,64]{1,3,0,2:T(8,128)} %bitcast.12) | data formatting | bytes 37748736 | tf_op jit(solution)/shard_map/transpose | solution.py:53
  383.1 359.8 %while.10 = (s32[]{:T(128)}, f32[3,2,1536,512]{2,3,1,0:T(8,128)}, f32[3,2,1536,512]{2,3,1,0:T(8,128)}, pred[3]{0:T(512)(128)(4,1)S(1)}, f32[3,1536,1536]{2,1,0:T...) while((s32[]{:T(128)}, f32[3,2,1536,512]{2,3,1,0:T(8,128)}, ...), condition=%wide.region_1.2_spmd, body=%wide.region_0.1_spmd.sunk | while | flops 43498340352 | bytes 179310272 | solution.py:63
  403.5 8.1 dynamic-slice_bitcast_fusion.16
  411.5 9.6 copy.80
  421.8 22.7 %convolution_multiply_fusion.3 = f32[1536,1536]{1,0:T(8,128)S(1)} fusion(f32[1536,1536]{0,1:T(8,128)} %copy.80, pred[]{:T(512)} %bitcast.83, f32[3,2,1536,512]{2,3,1,0:T(8,128)} %get-tuple-element.113, s32[]{:T(128)} %get-tuple-element.101, s32[]{:T(128)S(6)} %add.54, f32[3,1536,1536]{2,1,0:T(8,128)} %get-tuple-element.115), kind=kOutput, calls=%fused_computation.1.clone.1 | convolution fusion | flops 14504951808 | bytes 34605060 | tf_op jit(solution)/shard_map/while/body/eval_jaxpr/dot_general | solution.py:8
  448.0 17.0 %convolution_bitcast_fusion.2 = f32[1,1536,512]{2,1,0:T(8,128)S(1)} fusion(f32[1536,1536]{1,0:T(8,128)S(1)} %convolution_multiply_fusion.3, f32[3,2,1536,512]{2,3,1,0:T(8,128)} %get-tuple-element.113, s32[]{:T(128)} %get-tuple-element.101, s32[]{:T(128)S(6)} %add.54), kind=kOutput, calls=%fused_computation.9.clone.1 | convolution fusion | flops 14495514624 | bytes 15729156 | tf_op jit(solution)/shard_map/while/body/eval_jaxpr/dot_general | solution.py:16
  465.6 32.9 %fusion.22 = f32[1,1536,512]{2,1,0:T(8,128)S(1)} fusion(f32[1536,1536]{1,0:T(8,128)} %copy-done, f32[3,2,1536,512]{2,3,1,0:T(8,128)} %get-tuple-element.113, s32[]{:T(128)} %get-tuple-element.101, f32[]{:T(128)S(6)} %select_n.60), kind=kOutput, calls=%fused_computation.8.clone.1 | convolution fusion | flops 14496301056 | bytes 15729156 | tf_op jit(solution)/shard_map/while/body/eval_jaxpr/dot_general | solution.py:19
  501.8 6.6 copy.81
  514.3 8.1 dynamic-slice_bitcast_fusion.16
  522.3 9.6 copy.80
  532.5 22.7 %convolution_multiply_fusion.3 = f32[1536,1536]{1,0:T(8,128)S(1)} fusion(f32[1536,1536]{0,1:T(8,128)} %copy.80, pred[]{:T(512)} %bitcast.83, f32[3,2,1536,512]{2,3,1,0:T(8,128)} %get-tuple-element.113, s32[]{:T(128)} %get-tuple-element.101, s32[]{:T(128)S(6)} %add.54, f32[3,1536,1536]{2,1,0:T(8,128)} %get-tuple-element.115), kind=kOutput, calls=%fused_computation.1.clone.1 | convolution fusion | flops 14504951808 | bytes 34605060 | tf_op jit(solution)/shard_map/while/body/eval_jaxpr/dot_general | solution.py:8
  558.8 17.0 %convolution_bitcast_fusion.2 = f32[1,1536,512]{2,1,0:T(8,128)S(1)} fusion(f32[1536,1536]{1,0:T(8,128)S(1)} %convolution_multiply_fusion.3, f32[3,2,1536,512]{2,3,1,0:T(8,128)} %get-tuple-element.113, s32[]{:T(128)} %get-tuple-element.101, s32[]{:T(128)S(6)} %add.54), kind=kOutput, calls=%fused_computation.9.clone.1 | convolution fusion | flops 14495514624 | bytes 15729156 | tf_op jit(solution)/shard_map/while/body/eval_jaxpr/dot_general | solution.py:16
  576.4 32.9 %fusion.22 = f32[1,1536,512]{2,1,0:T(8,128)S(1)} fusion(f32[1536,1536]{1,0:T(8,128)} %copy-done, f32[3,2,1536,512]{2,3,1,0:T(8,128)} %get-tuple-element.113, s32[]{:T(128)} %get-tuple-element.101, f32[]{:T(128)S(6)} %select_n.60), kind=kOutput, calls=%fused_computation.8.clone.1 | convolution fusion | flops 14496301056 | bytes 15729156 | tf_op jit(solution)/shard_map/while/body/eval_jaxpr/dot_general | solution.py:19
  625.1 8.1 dynamic-slice_bitcast_fusion.16
  633.2 9.6 copy.80
  643.4 22.7 %convolution_multiply_fusion.3 = f32[1536,1536]{1,0:T(8,128)S(1)} fusion(f32[1536,1536]{0,1:T(8,128)} %copy.80, pred[]{:T(512)} %bitcast.83, f32[3,2,1536,512]{2,3,1,0:T(8,128)} %get-tuple-element.113, s32[]{:T(128)} %get-tuple-element.101, s32[]{:T(128)S(6)} %add.54, f32[3,1536,1536]{2,1,0:T(8,128)} %get-tuple-element.115), kind=kOutput, calls=%fused_computation.1.clone.1 | convolution fusion | flops 14504951808 | bytes 34605060 | tf_op jit(solution)/shard_map/while/body/eval_jaxpr/dot_general | solution.py:8
  669.7 17.0 %convolution_bitcast_fusion.2 = f32[1,1536,512]{2,1,0:T(8,128)S(1)} fusion(f32[1536,1536]{1,0:T(8,128)S(1)} %convolution_multiply_fusion.3, f32[3,2,1536,512]{2,3,1,0:T(8,128)} %get-tuple-element.113, s32[]{:T(128)} %get-tuple-element.101, s32[]{:T(128)S(6)} %add.54), kind=kOutput, calls=%fused_computation.9.clone.1 | convolution fusion | flops 14495514624 | bytes 15729156 | tf_op jit(solution)/shard_map/while/body/eval_jaxpr/dot_general | solution.py:16
  687.2 32.9 %fusion.22 = f32[1,1536,512]{2,1,0:T(8,128)S(1)} fusion(f32[1536,1536]{1,0:T(8,128)} %copy-done, f32[3,2,1536,512]{2,3,1,0:T(8,128)} %get-tuple-element.113, s32[]{:T(128)} %get-tuple-element.101, f32[]{:T(128)S(6)} %select_n.60), kind=kOutput, calls=%fused_computation.8.clone.1 | convolution fusion | flops 14496301056 | bytes 15729156 | tf_op jit(solution)/shard_map/while/body/eval_jaxpr/dot_general | solution.py:19
  742.9 12.6 %copy.60 = f32[8,6,1536,64]{2,3,1,0:T(8,128)} copy(f32[8,6,1536,64]{2,3,0,1:T(8,128)} %bitcast.87) | data formatting | bytes 37748736 | tf_op jit(solution)/shard_map/transpose | solution.py:64
  755.5 210.7 %all_to_all.10 = f32[8,6,1536,64]{2,3,1,0:T(8,128)S(1)} all-to-all(f32[8,6,1536,64]{2,3,1,0:T(8,128)} %copy.60), channel_id=1, replica_groups=mesh['grp'=4,'band'=8] {'band'}, dimensions={0} | all-to-all | bytes 37748736 | tf_op jit(solution)/shard_map/all_to_all | solution.py:65
  966.3 15.2 %fusion.8 = f32[12,1536,64]{1,0,2:T(8,128)} fusion(f32[8,6,1536,64]{2,3,1,0:T(8,128)S(1)} %all_to_all.10, s32[8,6]{0,1:T(8,128)S(1)} %copy-done.5), kind=kOutput, calls=%fused_computation.19 | convolution fusion | flops 679477824 | bytes 23593152 | tf_op jit(solution)/shard_map/srk,srpc->kpc/dot_general | solution.py:69
  981.5 11.0 reshape.57
  992.5 12.2 %copy.63 = f32[12,4,8,48,64]{4,3,2,0,1:T(8,128)} copy(f32[12,4,8,48,64]{3,2,1,0,4:T(8,128)} %reshape.57) | data formatting | bytes 9437184 | tf_op jit(solution)/shard_map/reshape | solution.py:70
  1004.8 157.8 %reduce-scatter.2.cloned.1.call-done = f32[12,1,8,48,64]{4,3,2,0,1:T(8,128)} async-done(((f32[12,4,8,48,64]{4,3,2,0,1:T(8,128)}), f32[12,1,8,48,64]{4,3,2,0,1:T(8,128)}) %reduce-scatter.2.cloned.1.call-update) | async-done | bytes 1179664 | tf_op jit(solution)/shard_map/reduce_scatter | solution.py:71
  (62 shorter events, 88.4 us)
Async XLA Ops:
  6.5 31.2 %collective-permute-start = (f32[4608,64]{0,1:T(8,128)}, f32[4608,64]{0,1:T(8,128)S(1)}, u32[]{:S(2)}, u32[]{:S(2)}) collective-permute-start(f32[4608,64]{0,1:T(8,128)} %param.5), channel_id=1, source_target_pairs={{0,8},{8,16},{16,24},{24,0},{1,9},{9,17},{17,25},{25,1},{2,10},{10... | collective-permute-start | bytes 3538952 | tf_op jit(solution)/shard_map/ppermute | solution.py:36
  37.8 29.1 %collective-permute-start.1 = (f32[4608,64]{0,1:T(8,128)S(1)}, f32[4608,64]{0,1:T(8,128)}, u32[]{:S(2)}, u32[]{:S(2)}) collective-permute-start(f32[4608,64]{0,1:T(8,128)S(1)} %collective-permute-done), channel_id=1, source_target_pairs={{0,8},{8,16},{16,24},{24,0},{1,9},{9,17},{17,25},{25,1},{2,10},{10... | collective-permute-start | bytes 3538952 | tf_op jit(solution)/shard_map/ppermute | solution.py:36
  66.8 28.3 %collective-permute-start.2 = (f32[4608,64]{0,1:T(8,128)}, f32[4608,64]{0,1:T(8,128)}, u32[]{:S(2)}, u32[]{:S(2)}) collective-permute-start(f32[4608,64]{0,1:T(8,128)} %collective-permute-done.1), channel_id=1, source_target_pairs={{0,8},{8,16},{16,24},{24,0},{1,9},{9,17},{17,25},{25,1},{2,10},{10... | collective-permute-start | bytes 3538952 | tf_op jit(solution)/shard_map/ppermute | solution.py:36
  70.0 32.0 %copy-start.4 = (s32[8,6]{0,1:T(8,128)}, s32[8,6]{0,1:T(8,128)S(1)}, u32[]{:S(2)}) copy-start(s32[8,6]{0,1:T(8,128)S(1)} %get-tuple-element.59) | copy-start | bytes 580
  98.0 4.0 copy-start.1
  98.0 4.3 copy-start.3
  100.0 2.8 copy-start.2
  158.1 6.1 copy-start.6
  158.1 212.4 %all-to-all-start = ((f32[8,6,1536,64]{2,3,1,0:T(8,128)}), f32[8,6,1536,64]{2,3,1,0:T(8,128)}, u32[]{:S(2)}, u32[]{:S(2)}) async-start(f32[8,6,1536,64]{2,3,1,0:T(8,128)} %select_multiply_fusion), calls=%async_computation | async-start | bytes 37748736 | tf_op jit(solution)/shard_map/all_to_all | solution.py:52
  164.1 998.4 %reduce-scatter.2.cloned.1.call-start = ((), (), s32[]{:S(2)}) async-start(), calls=%async_computation.3 | async-start | bytes 11796480 | tf_op jit(solution)/shard_map/reduce_scatter | solution.py:71
  444.4 3.6 copy-start
  555.2 3.6 copy-start
  666.1 3.6 copy-start
  755.5 210.7 %copy-start.5 = (s32[8,6]{0,1:T(8,128)S(1)}, s32[8,6]{0,1:T(8,128)}, u32[]{:S(2)}) copy-start(s32[8,6]{0,1:T(8,128)} %copy-done.4) | copy-start | bytes 580
Sparse Core Ops, SparseCore 0:
  1004.9 157.6 reduce-scatter.1
